TPU v7x, 256 devices: a whole 4x4x8 slice. The times are simulated.
256 devices in a mesh: feat: 8 (over x, core), rows: 32 (over y, z).
Axes of the slice: x: 4, y: 4, z: 8, core: 2. Of those that a mesh axis runs over, the one named last changes fastest.
Arguments:
- kernel: float32 [8192, 8192], P('rows', 'feat'), may hold values from -0.06629126 to 5, as said below
- train_feats: float32 [16384, 8192], P('rows', 'feat'), may hold values from -6 to 6
- test_feats: float32 [8192, 8192], P('rows', 'feat'), may hold values from -6 to 6
Outputs:
- factor_state: float32 [8192, 8192], P('rows', 'feat')
- train_state: float32 [16384, 8192], P('rows', 'feat')
- test_state: float32 [8192, 8192], P('rows', 'feat')
- scores: float32 [16384, 8192], P('rows', 'feat')
Inputs may be any that keep to these rules, and one draw needn't show every extreme that they name: kernel is symmetric and positive definite; its diagonal dominates each row's other entries.
All inputs are finite; a program needn't handle non-finite values.
Results may differ from a plain program's by a relative error of at most 0.0001.
Values sent between devices are 32-bit elements; how exact they have to be, the bound alone decides.
No kernel may reach another device: no remote copies, remote signals or barrier semaphores. Data moves between devices by JAX's collectives and lax.ppermute only.
A program may use at most 128 MiB of HBM per device.

v0:
```python
import jax
import jax.numpy as jnp
from jax import lax
from jax.sharding import PartitionSpec as P

PANEL = 256
NPAN = 2


def from_root(block, axis, holder):
    block = jnp.where(lax.axis_index(axis) == holder, block, jnp.zeros_like(block))
    return lax.psum(block, axis)


def product(left, right):
    return jnp.dot(left, right, precision=lax.Precision.HIGHEST, preferred_element_type=jnp.float32)


def update_state(state, coords, right_rows):
    return state - product(coords, right_rows.T)


def per_device(kernel, train_feats, test_feats):
    blk_rows, blk_cols = kernel.shape
    row_index = lax.axis_index("rows")
    feat_index = lax.axis_index("feat")
    row_ids = row_index * blk_rows + jnp.arange(blk_rows, dtype=jnp.int32)
    col_ids = feat_index * blk_cols + jnp.arange(blk_cols, dtype=jnp.int32)
    on_panel = feat_index == 0
    identity = jnp.eye(PANEL, dtype=jnp.float32)
    matrix, train_work, test_work = (kernel, train_feats, test_feats)
    train_parts = []
    test_parts = []
    pending = None
    for panel in range(NPAN):
        first_col = panel * PANEL
        last_col = first_col + PANEL
        root_row = first_col // blk_rows
        pending = (
            matrix[:, first_col:last_col],
            matrix,
            train_work[:, first_col:last_col],
            test_work[:, first_col:last_col],
        )
        col_block, row_block, train_block, test_block = pending
        diagonal = from_root(col_block, ("feat", "rows"), root_row)
        factor = jnp.linalg.cholesky(diagonal)
        transposed = jax.scipy.linalg.solve_triangular(factor, identity, lower=True).T
        left_rows = jnp.where((row_ids >= first_col)[:, None], product(col_block, transposed), 0.0)
        train_coords = product(train_block, transposed)
        test_coords = product(test_block, transposed)
        left_rows, train_coords, test_coords = (
            from_root(left_rows, "feat", 0),
            from_root(train_coords, "feat", 0),
            from_root(test_coords, "feat", 0),
        )
        right_rows = jnp.where(
            (col_ids >= first_col)[:, None], product(row_block.T, transposed), 0.0
        )
        right_rows = from_root(right_rows, "rows", root_row)
        train_parts.append(train_coords)
        test_parts.append(test_coords)
        pending = None
        matrix = update_state(matrix, left_rows, right_rows)
        matrix = matrix.at[:, first_col:last_col].set(
            jnp.where(on_panel, left_rows, matrix[:, first_col:last_col])
        )
        train_work = update_state(train_work, train_coords, right_rows)
        train_work = train_work.at[:, first_col:last_col].set(
            jnp.where(on_panel, train_coords, train_work[:, first_col:last_col])
        )
        test_work = update_state(test_work, test_coords, right_rows)
        test_work = test_work.at[:, first_col:last_col].set(
            jnp.where(on_panel, test_coords, test_work[:, first_col:last_col])
        )
    coord_span = NPAN * PANEL
    upper = (row_ids[:, None] < coord_span) & (col_ids[None, :] >= coord_span)
    matrix = jnp.where(upper, 0.0, matrix)
    train_all = jnp.concatenate(train_parts, axis=1)
    test_all = jnp.concatenate(test_parts, axis=1)
    groups = lax.axis_size("rows") // lax.axis_size("feat")
    every_test = lax.all_gather(test_all, "rows", axis=0, tiled=True)
    wanted = lax.dynamic_slice_in_dim(
        every_test, feat_index * (groups * test_all.shape[0]), groups * test_all.shape[0], 0
    )
    scores = product(train_all, wanted.T)
    return (matrix, train_work, test_work, scores)


def solution(mesh):
    return jax.shard_map(
        per_device,
        mesh=mesh,
        in_specs=(P("rows", "feat"), P("rows", "feat"), P("rows", "feat")),
        out_specs=(P("rows", "feat"), P("rows", "feat"), P("rows", "feat"), P("rows", "feat")),
        check_vma=False,
    )
```

profile of v0, /device:TPU:2, one launch (start us, length us, event | category | flops | bytes accessed | tf_op | source)
XLA Modules:
  0.0 1282.0 jit_solution(15849999229756976496)
XLA Ops:
  7.2 1.6 copy.13
  9.6 261.8 %all-reduce.10.cloned.1.call-done = f32[256,256]{0,1:T(8,128)} async-done(((f32[256,256]{0,1:T(8,128)}), f32[256,256]{0,1:T(8,128)}) %all-reduce.10.cloned.1.call-update) | async-done | bytes 262160 | tf_op jit(solution)/shard_map/psum | solution.py:12
  273.6 11.7 cholesky.130
  285.3 9.8 custom-call.13
  295.6 11.7 cholesky.147
  309.4 4.5 while.10
  310.6 1.4 bitcast_dynamic-update-slice_fusion.4
  312.6 1.4 bitcast_dynamic-update-slice_fusion.4
  314.0 19.7 %custom-call.14 = f32[2,128,128]{1,2,0:T(8,128)S(1)} custom-call(f32[2,128,128]{2,1,0:T(8,128)S(1)} %get-tuple-element.92), custom_call_target="InvertDiagBlocksLowerTriangular" | custom-call | tf_op jit(solution)/shard_map/jit(_solve_triangular)/triangular_solve | solution.py:48
  335.7 1.4 fusion.6
  337.9 2.5 fusion.5
  340.4 2.8 fusion.4
  343.4 2.5 copy.24
  345.9 2.9 copy.18
  349.4 55.5 %all-reduce.20.cloned.1.call-done = (f32[256,256]{0,1:T(8,128)}, f32[512,256]{0,1:T(8,128)}, f32[256,256]{0,1:T(8,128)}) async-done(((f32[256,256]{0,1:T(8,128)}, f32[512,256]{0,1:T(8,128)}, f32[256,256]{0,1:T(8,128)}), (f32[256,256]{0,1:T(8,128)}, f32[512,256]{0,1:T(8,128)}, f32[256,256]{0,1:T(8,128)})) %all-reduce.20.cloned.1.call-update) | async-done | bytes 1048592 | tf_op jit(solution)/shard_map/psum | solution.py:12
  404.9 156.3 %all-reduce.12.cloned.1.call-done = f32[1024,256]{1,0:T(8,128)} async-done(((f32[1024,256]{1,0:T(8,128)}), f32[1024,256]{1,0:T(8,128)}) %all-reduce.12.cloned.1.call-update) | async-done | bytes 1048592 | tf_op jit(solution)/shard_map/psum | solution.py:12
  561.2 2.3 convolution_subtract_fusion.5
  565.2 4.0 convolution_subtract_fusion.1
  570.5 2.0 convolution_subtract_fusion.3
  572.4 2.2 fusion.19
  574.7 244.1 %all-reduce.14.cloned.1.call-done = f32[256,256]{0,1:T(8,128)} async-done(((f32[256,256]{0,1:T(8,128)}), f32[256,256]{0,1:T(8,128)}) %all-reduce.14.cloned.1.call-update) | async-done | bytes 262160 | tf_op jit(solution)/shard_map/psum | solution.py:12
  818.8 1.8 copy.15
  822.3 11.7 cholesky.164
  834.8 10.4 custom-call.15
  846.0 1.7 constant_dynamic-update-slice_fusion
  848.8 11.9 cholesky.181
  863.3 1.7 select_select_fusion.6
  865.0 5.8 while.11
  865.6 2.3 bitcast_dynamic-update-slice_fusion.5
  868.5 2.2 bitcast_dynamic-update-slice_fusion.5
  870.8 20.3 %custom-call.16 = f32[2,128,128]{1,2,0:T(8,128)} custom-call(f32[2,128,128]{2,1,0:T(8,128)S(1)} %get-tuple-element.93), custom_call_target="InvertDiagBlocksLowerTriangular" | custom-call | tf_op jit(solution)/shard_map/jit(_solve_triangular)/triangular_solve | solution.py:48
  893.3 1.2 fusion.33
  895.6 2.1 convolution_select_fusion.4
  897.7 1.4 convolution_select_fusion.2
  899.2 2.0 fusion.2
  901.5 62.1 %all-reduce.18.cloned.1.call-done = (f32[256,256]{0,1:T(8,128)}, f32[512,256]{0,1:T(8,128)}, f32[256,256]{0,1:T(8,128)}) async-done(((f32[256,256]{0,1:T(8,128)}, f32[512,256]{0,1:T(8,128)}, f32[256,256]{0,1:T(8,128)}), (f32[256,256]{0,1:T(8,128)}, f32[512,256]{0,1:T(8,128)}, f32[256,256]{0,1:T(8,128)})) %all-reduce.18.cloned.1.call-update) | async-done | bytes 1048592 | tf_op jit(solution)/shard_map/psum | solution.py:12
  963.6 1.9 pad_maximum_fusion
  966.2 153.6 %all-reduce.16.cloned.1.call-done = f32[1024,256]{1,0:T(8,128)} async-done(((f32[1024,256]{1,0:T(8,128)}), f32[1024,256]{1,0:T(8,128)}) %all-reduce.16.cloned.1.call-update) | async-done | bytes 1048592 | tf_op jit(solution)/shard_map/psum | solution.py:12
  1119.8 2.3 convolution_subtract_fusion.4
  1122.8 1.2 and_select_fusion
  1124.0 2.5 copy.28
  1126.5 4.3 convolution_subtract_fusion
  1130.8 2.5 fusion.14
  1133.3 3.0 copy.29
  1136.3 2.2 convolution_subtract_fusion.2
  1139.3 1.3 copy.30
  1140.6 127.8 %all-gather.2.cloned.1.call-done = f32[8192,512]{0,1:T(8,128)} async-done(((f32[256,512]{0,1:T(8,128)}), f32[8192,512]{0,1:T(8,128)}) %all-gather.2.cloned.1.call-update) | async-done | bytes 16777232 | tf_op jit(solution)/shard_map/all_gather | solution.py:82
  1268.4 6.4 fusion
  (93 shorter events, 24.3 us)
Async XLA Ops:
  7.2 264.3 %all-reduce.10.cloned.1.call-start = ((), (), s32[]{:S(2)}) async-start(), calls=%async_computation | async-start | bytes 524288 | tf_op jit(solution)/shard_map/psum | solution.py:12
  9.5 395.3 %all-reduce.20.cloned.1.call-start = ((), (), s32[]{:S(2)}) async-start(), calls=%async_computation.6 | async-start | bytes 2097152 | tf_op jit(solution)/shard_map/psum | solution.py:12
  334.6 5.9 copy-start.6
  340.3 220.9 %all-reduce.12.cloned.1.call-start = ((), (), s32[]{:S(2)}) async-start(), calls=%async_computation.1 | async-start | bytes 2097152 | tf_op jit(solution)/shard_map/psum | solution.py:12
  343.3 475.5 %all-reduce.14.cloned.1.call-start = ((), (), s32[]{:S(2)}) async-start(), calls=%async_computation.2 | async-start | bytes 524288 | tf_op jit(solution)/shard_map/psum | solution.py:12
  404.9 158.7 %copy-start.11 = (f32[256,256]{0,1:T(8,128)S(1)}, f32[256,256]{0,1:T(8,128)}, u32[]{:S(2)}) copy-start(f32[256,256]{0,1:T(8,128)} %get-tuple-element.117) | copy-start | bytes 786436
  564.9 398.7 %all-reduce.18.cloned.1.call-start = ((), (), s32[]{:S(2)}) async-start(), calls=%async_computation.5 | async-start | bytes 2097152 | tf_op jit(solution)/shard_map/psum | solution.py:12
  565.1 4.1 copy-start.2
  565.1 4.9 copy-start.7
  565.2 4.9 copy-start.8
  569.2 1.2 copy-start.1
  821.6 0.7 copy-start.12
  899.1 220.7 %all-reduce.16.cloned.1.call-start = ((), (), s32[]{:S(2)}) async-start(), calls=%async_computation.3 | async-start | bytes 2097152 | tf_op jit(solution)/shard_map/psum | solution.py:12
  901.2 367.2 %all-gather.2.cloned.1.call-start = ((), (), s32[]{:S(2)}) async-start(), calls=%async_computation.4 | async-start | bytes 17301504 | tf_op jit(solution)/shard_map/all_gather | solution.py:82
  965.5 156.6 %copy-start.10 = (f32[256,256]{0,1:T(8,128)S(1)}, f32[256,256]{0,1:T(8,128)}, u32[]{:S(2)}) copy-start(f32[256,256]{0,1:T(8,128)} %get-tuple-element.114) | copy-start | bytes 786436
  1122.8 3.7 copy-start
  1126.5 4.3 copy-start.4
  1133.3 3.0 copy-start.9
  1138.5 129.8 %copy-start.3 = (f32[512,256]{0,1:T(8,128)S(1)}, f32[512,256]{0,1:T(8,128)}, u32[]{:S(2)}) copy-start(f32[512,256]{0,1:T(8,128)} %get-tuple-element.118) | copy-start | bytes 1572868
  1138.5 129.8 %copy-start.5 = (f32[512,256]{0,1:T(8,128)S(1)}, f32[512,256]{0,1:T(8,128)}, u32[]{:S(2)}) copy-start(f32[512,256]{0,1:T(8,128)} %get-tuple-element.115) | copy-start | bytes 1572868
Sparse Core Ops, SparseCore 0:
  14.0 257.4 all-reduce.9
  340.5 64.3 all-reduce.19
  408.9 152.2 all-reduce.11
  567.1 251.6 all-reduce.13
  899.2 64.3 all-reduce.17
  967.5 152.2 all-reduce.15
  1122.3 146.0 all-gather.1
where the time goes:
time: 1290 us; the launch traced here: 1280 us
  waiting for transfers between devices  1060 us (82%)
  other arithmetic  127 us (10%)
  matrix products  45.5 us (4%)
  local copies, waits for them, and re-layouts  29.1 us (2%)
  between operations  17.6 us (1%)
    psum x6, waiting for transfers between devices, from_root(): return lax.psum(block, axis)  933 us
    all_gather x1, waiting for transfers between devices, per_device(): every_test = lax.all_gather(test_all, 'rows', axis=0, tiled=True)  128 us
    another operation x13, other arithmetic, per_device(): factor = jnp.linalg.cholesky(diagonal)  70 us
    another operation x5, other arithmetic, per_device(): jax.scipy.linalg.solve_triangular(factor, identity, lower=True)  41.7 us
    dot_general x15, matrix products, product(): jnp.dot(left, right, precision=lax.Precision.HIGHEST, preferred_element_t...  38 us
  transfers between devices with their start and end apart: 7, of which 7 were waited for; matrix products, arithmetic and copies ran while one was open for 3% of the time, Pallas kernels for 0%

commit v1 on v0

--- a/solution.py
+++ b/solution.py
@@ -79,7 +79,9 @@
     train_all = jnp.concatenate(train_parts, axis=1)
     test_all = jnp.concatenate(test_parts, axis=1)
     groups = lax.axis_size("rows") // lax.axis_size("feat")
-    every_test = lax.all_gather(test_all, "rows", axis=0, tiled=True)
+    every_test = jnp.concatenate(
+        lax.all_to_all(jnp.stack([test_all] * lax.axis_size("rows")), "rows", 0, 0), axis=0
+    )
     wanted = lax.dynamic_slice_in_dim(
         every_test, feat_index * (groups * test_all.shape[0]), groups * test_all.shape[0], 0
     )

time: 1290 us -> 1440 us (1.12)
  the two profiles are of different devices: /device:TPU:2 before, /device:TPU:15 now
where the time goes in v1:
time: 1440 us; the launch traced here: 1430 us
  waiting for transfers between devices  1190 us (83%)
  other arithmetic  128 us (9%)
  matrix products  48.7 us (3%)
  local copies, waits for them, and re-layouts  39.9 us (3%)
  between operations  17.3 us (1%)
    psum x6, waiting for transfers between devices, from_root(): return lax.psum(block, axis)  1100 us
    all_to_all x1, waiting for transfers between devices, per_device(): lax.all_to_all(jnp.stack([test_all] * lax.axis_size('rows')), 'rows', 0, 0)  90.7 us
    another operation x13, other arithmetic, per_device(): factor = jnp.linalg.cholesky(diagonal)  70.2 us
    another operation x5, other arithmetic, per_device(): jax.scipy.linalg.solve_triangular(factor, identity, lower=True)  41.7 us
    dot_general x15, matrix products, product(): jnp.dot(left, right, precision=lax.Precision.HIGHEST, preferred_element_t...  41.1 us
  transfers between devices with their start and end apart: 7, of which 7 were waited for; matrix products, arithmetic and copies ran while one was open for 3% of the time, Pallas kernels for 0%

profile of v1, /device:TPU:15, one launch (start us, length us, event | category | flops | bytes accessed | tf_op | source)
XLA Modules:
  0.0 1432.4 jit_solution(5135429283169273853)
XLA Ops:
  7.2 1.6 copy.13
  9.6 260.0 %all-reduce.10.cloned.1.call-done = f32[256,256]{0,1:T(8,128)} async-done(((f32[256,256]{0,1:T(8,128)}), f32[256,256]{0,1:T(8,128)}) %all-reduce.10.cloned.1.call-update) | async-done | bytes 262160 | tf_op jit(solution)/shard_map/psum | solution.py:12
  271.7 11.7 cholesky.130
  283.5 9.8 custom-call.13
  293.8 11.7 cholesky.147
  307.6 4.2 while.10
  308.4 1.4 bitcast_dynamic-update-slice_fusion.4
  310.4 1.4 bitcast_dynamic-update-slice_fusion.4
  311.8 19.7 %custom-call.14 = f32[2,128,128]{1,2,0:T(8,128)S(1)} custom-call(f32[2,128,128]{2,1,0:T(8,128)S(1)} %get-tuple-element.92), custom_call_target="InvertDiagBlocksLowerTriangular" | custom-call | tf_op jit(solution)/shard_map/jit(_solve_triangular)/triangular_solve | solution.py:48
  333.5 1.4 fusion.6
  335.7 2.5 fusion.5
  338.3 2.8 fusion.4
  341.2 2.5 copy.24
  343.7 2.9 copy.18
  347.3 58.3 %all-reduce.20.cloned.1.call-done = (f32[256,256]{0,1:T(8,128)}, f32[512,256]{0,1:T(8,128)}, f32[256,256]{0,1:T(8,128)}) async-done(((f32[256,256]{0,1:T(8,128)}, f32[512,256]{0,1:T(8,128)}, f32[256,256]{0,1:T(8,128)}), (f32[256,256]{0,1:T(8,128)}, f32[512,256]{0,1:T(8,128)}, f32[256,256]{0,1:T(8,128)})) %all-reduce.20.cloned.1.call-update) | async-done | bytes 1048592 | tf_op jit(solution)/shard_map/psum | solution.py:12
  405.6 149.1 %all-reduce.12.cloned.1.call-done = f32[1024,256]{1,0:T(8,128)} async-done(((f32[1024,256]{1,0:T(8,128)}), f32[1024,256]{1,0:T(8,128)}) %all-reduce.12.cloned.1.call-update) | async-done | bytes 1048592 | tf_op jit(solution)/shard_map/psum | solution.py:12
  554.7 2.3 convolution_subtract_fusion.5
  558.8 4.0 convolution_subtract_fusion.1
  564.1 2.0 convolution_subtract_fusion.3
  566.0 2.3 fusion.19
  568.3 248.2 %all-reduce.14.cloned.1.call-done = f32[256,256]{0,1:T(8,128)} async-done(((f32[256,256]{0,1:T(8,128)}), f32[256,256]{0,1:T(8,128)}) %all-reduce.14.cloned.1.call-update) | async-done | bytes 262160 | tf_op jit(solution)/shard_map/psum | solution.py:12
  816.6 1.8 copy.15
  820.1 11.7 cholesky.164
  832.5 10.4 custom-call.15
  843.7 1.7 constant_dynamic-update-slice_fusion
  846.5 12.1 cholesky.181
  861.2 1.7 select_select_fusion.6
  862.9 5.8 while.11
  863.5 2.3 bitcast_dynamic-update-slice_fusion.5
  866.4 2.2 bitcast_dynamic-update-slice_fusion.5
  868.6 20.3 %custom-call.16 = f32[2,128,128]{1,2,0:T(8,128)} custom-call(f32[2,128,128]{2,1,0:T(8,128)S(1)} %get-tuple-element.93), custom_call_target="InvertDiagBlocksLowerTriangular" | custom-call | tf_op jit(solution)/shard_map/jit(_solve_triangular)/triangular_solve | solution.py:48
  893.5 2.0 convolution_select_fusion.4
  895.5 1.4 convolution_select_fusion.2
  897.0 67.4 %all-reduce.18.cloned.1.call-done = (f32[256,256]{0,1:T(8,128)}, f32[512,256]{0,1:T(8,128)}, f32[256,256]{0,1:T(8,128)}) async-done(((f32[256,256]{0,1:T(8,128)}, f32[512,256]{0,1:T(8,128)}, f32[256,256]{0,1:T(8,128)}), (f32[256,256]{0,1:T(8,128)}, f32[512,256]{0,1:T(8,128)}, f32[256,256]{0,1:T(8,128)})) %all-reduce.18.cloned.1.call-update) | async-done | bytes 1048592 | tf_op jit(solution)/shard_map/psum | solution.py:12
  964.4 1.9 pad_maximum_fusion
  966.2 2.0 copy.28
  968.3 8.9 stack.2
  977.2 9.7 all-to-all-start
  986.9 2.0 fusion.2
  989.8 314.3 %all-reduce.16.cloned.1.call-done = f32[1024,256]{1,0:T(8,128)} async-done(((f32[1024,256]{1,0:T(8,128)}), f32[1024,256]{1,0:T(8,128)}) %all-reduce.16.cloned.1.call-update) | async-done | bytes 1048592 | tf_op jit(solution)/shard_map/psum | solution.py:12
  1304.1 2.3 convolution_subtract_fusion.4
  1308.3 2.5 copy.29
  1310.9 4.3 convolution_subtract_fusion
  1315.2 2.6 fusion.14
  1317.7 2.9 copy.30
  1320.7 2.2 convolution_subtract_fusion.2
  1325.0 90.7 %all-to-all-done = f32[32,256,512]{2,1,0:T(8,128)} async-done(((f32[32,256,512]{2,1,0:T(8,128)}), f32[32,256,512]{2,1,0:T(8,128)}, u32[]{:S(2)}, u32[]{:S(2)}) %all-to-all-start) | async-done | bytes 16777248 | tf_op jit(solution)/shard_map/all_to_all | solution.py:83
  1415.8 9.6 fusion
  (94 shorter events, 28.1 us)
Async XLA Ops:
  7.2 262.5 %all-reduce.10.cloned.1.call-start = ((), (), s32[]{:S(2)}) async-start(), calls=%async_computation.1 | async-start | bytes 524288 | tf_op jit(solution)/shard_map/psum | solution.py:12
  9.5 396.1 %all-reduce.20.cloned.1.call-start = ((), (), s32[]{:S(2)}) async-start(), calls=%async_computation.6 | async-start | bytes 2097152 | tf_op jit(solution)/shard_map/psum | solution.py:12
  332.4 5.9 copy-start.6
  338.2 216.5 %all-reduce.12.cloned.1.call-start = ((), (), s32[]{:S(2)}) async-start(), calls=%async_computation.2 | async-start | bytes 2097152 | tf_op jit(solution)/shard_map/psum | solution.py:12
  341.1 475.4 %all-reduce.14.cloned.1.call-start = ((), (), s32[]{:S(2)}) async-start(), calls=%async_computation.3 | async-start | bytes 524288 | tf_op jit(solution)/shard_map/psum | solution.py:12
  405.6 151.4 %copy-start.11 = (f32[256,256]{0,1:T(8,128)S(1)}, f32[256,256]{0,1:T(8,128)}, u32[]{:S(2)}) copy-start(f32[256,256]{0,1:T(8,128)} %get-tuple-element.117) | copy-start | bytes 786436
  558.5 405.9 %all-reduce.18.cloned.1.call-start = ((), (), s32[]{:S(2)}) async-start(), calls=%async_computation.5 | async-start | bytes 2097152 | tf_op jit(solution)/shard_map/psum | solution.py:12
  558.7 4.1 copy-start.2
  558.7 5.0 copy-start.7
  558.7 5.0 copy-start.8
  562.8 1.2 copy-start
  819.4 0.7 copy-start.12
  977.2 438.6 %all-to-all-start = ((f32[32,256,512]{2,1,0:T(8,128)}), f32[32,256,512]{2,1,0:T(8,128)}, u32[]{:S(2)}, u32[]{:S(2)}) async-start(f32[32,256,512]{2,1,0:T(8,128)} %stack.2), calls=%async_computation | async-start | bytes 33554432 | tf_op jit(solution)/shard_map/all_to_all | solution.py:83
  986.9 317.2 %all-reduce.16.cloned.1.call-start = ((), (), s32[]{:S(2)}) async-start(), calls=%async_computation.4 | async-start | bytes 2097152 | tf_op jit(solution)/shard_map/psum | solution.py:12
  988.9 317.5 %copy-start.10 = (f32[256,256]{0,1:T(8,128)S(1)}, f32[256,256]{0,1:T(8,128)}, u32[]{:S(2)}) copy-start(f32[256,256]{0,1:T(8,128)} %get-tuple-element.114) | copy-start | bytes 786436
  1307.1 3.7 copy-start.1
  1310.9 4.3 copy-start.4
  1317.7 2.9 copy-start.9
  1322.9 92.9 %copy-start.3 = (f32[512,256]{0,1:T(8,128)S(1)}, f32[512,256]{0,1:T(8,128)}, u32[]{:S(2)}) copy-start(f32[512,256]{0,1:T(8,128)} %get-tuple-element.118) | copy-start | bytes 1572868
  1322.9 92.9 %copy-start.5 = (f32[512,256]{0,1:T(8,128)S(1)}, f32[512,256]{0,1:T(8,128)}, u32[]{:S(2)}) copy-start(f32[512,256]{0,1:T(8,128)} %get-tuple-element.115) | copy-start | bytes 1572868
Sparse Core Ops, SparseCore 0:
  14.0 255.5 all-reduce.9
  338.3 67.2 all-reduce.19
  409.6 145.0 all-reduce.11
  560.6 255.9 all-reduce.13
  897.1 67.2 all-reduce.17
  991.4 312.6 all-reduce.15
